TPU v7x, 128 devices: a whole 4x4x4 slice. The times are simulated.
128 devices in a mesh: pipe: 4 (over x_hi, core), dp: 16 (over y, z), tensor: 2 (over x_lo).
Axes of the slice: x: 4 (x_hi: 2, x_lo: 2; x = x_hi * 2 + x_lo), y: 4, z: 4, core: 2. Of those that a mesh axis runs over, the one named last changes fastest.
Arguments:
- hidden_states: bfloat16 [4, 4096, 8192], P('pipe', 'dp'), may hold values from -60 to 60
- norm_gain: bfloat16 [4, 8192], P('pipe'), may hold values from 0.5 to 2
- key_weight: bfloat16 [4, 8192, 512], P('pipe', 'dp', 'tensor'), may hold values from -0.0625 to 0.0625
- value_weight: bfloat16 [4, 8192, 512], P('pipe', 'dp', 'tensor'), may hold values from -0.0625 to 0.0625
- queries: bfloat16 [4, 4096, 4096], P('pipe', 'dp', 'tensor'), may hold values from -128 to 128
- context_cotangent: bfloat16 [4, 4096, 4096], P('pipe', 'dp', 'tensor'), may hold values from -96 to 96
- lengths: int32 [4, 16], P('pipe', 'dp'), may hold values from 64 to 256, as said below
- policy_logp: float32 [4, 16], P('pipe', 'dp'), may hold values from -90 to -30
- reference_logp: float32 [4, 16], P('pipe', 'dp'), may hold values from -90 to -30
Outputs:
- key_weight_grad: bfloat16 [4, 8192, 512], P('pipe', 'dp', 'tensor')
- value_weight_grad: bfloat16 [4, 8192, 512], P('pipe', 'dp', 'tensor')
- lower_cotangent: bfloat16 [4, 4096, 8192], P('pipe', 'dp')
Inputs may be any that keep to these rules, and one draw needn't show every extreme that they name: `lengths`: each sequence's live tokens; positions at or beyond it are padding.
All inputs are finite; a program needn't handle non-finite values.
Results may differ from a plain program's by a relative error of at most 0.015.
The roundings to bfloat16 on the way count: a program that leaves them out, or rounds other values in their place, can miss the bound.
Values may be sent and summed in bfloat16 or wider, within the bound.
No kernel may reach another device: no remote copies, remote signals or barrier semaphores. Data moves between devices by JAX's collectives and lax.ppermute only.
A program may use at most 128 MiB of HBM per device.

v0:
```python
import math
import jax
import jax.numpy as jnp
from jax import lax
from jax.sharding import PartitionSpec as P

HD = 128
npo_beta = 0.1
norm_eps = 1e-05
rope_base = 500000.0


def shifted(value, axis, steps):
    count = lax.axis_size(axis)
    leading, last = (max(0, -steps), min(count, count - steps))
    return lax.ppermute(value, axis, [(source, source + steps) for source in range(leading, last)])


def rope_tables(length, head_dim):
    positions = jnp.arange(length).astype(jnp.float32)
    freq_index = jnp.arange(head_dim // 2).astype(jnp.float32)
    inverse = 1.0 / rope_base ** (2.0 * freq_index / head_dim)
    angles = positions[:, None] * inverse[None, :]
    cosine = jnp.concatenate([jnp.cos(angles), jnp.cos(angles)], axis=1)
    sine = jnp.concatenate([jnp.sin(angles), jnp.sin(angles)], axis=1)
    return (cosine, sine)


def rotate_half(values):
    half = values.shape[-1] // 2
    return jnp.concatenate([-values[..., half:], values[..., :half]], axis=-1)


def rotate_back(values):
    half = values.shape[-1] // 2
    return jnp.concatenate([values[..., half:], -values[..., :half]], axis=-1)


def sequence_grads(query_seq, key_seq, value_seq, cotan_seq, length_seq, cosine, sine):
    seq_len, kv_heads, head_dim = key_seq.shape
    group = query_seq.shape[1] // kv_heads
    scale = 1.0 / math.sqrt(head_dim)
    query_g = query_seq.reshape(seq_len, kv_heads, group, head_dim)
    cotan_g = cotan_seq.reshape(seq_len, kv_heads, group, head_dim)
    scores = (
        jnp.einsum("ikgd,jkd->kgij", query_g, key_seq, preferred_element_type=jnp.float32) * scale
    )
    row_pos = jnp.arange(seq_len)[:, None]
    col_pos = jnp.arange(seq_len)[None, :]
    allowed = (col_pos <= row_pos) & (col_pos < length_seq)
    scores = jnp.where(allowed, scores, -1e30)
    highest = jnp.max(scores, axis=-1, keepdims=True)
    expd = jnp.where(allowed, jnp.exp(scores - highest), 0.0)
    probs = expd / jnp.sum(expd, axis=-1, keepdims=True)
    probs_low = probs.astype(jnp.bfloat16)
    value_grad = jnp.einsum(
        "kgij,ikgd->jkd", probs_low, cotan_g, preferred_element_type=jnp.float32
    ).astype(jnp.bfloat16)
    prob_grad = jnp.einsum("ikgd,jkd->kgij", cotan_g, value_seq, preferred_element_type=jnp.float32)
    centre = jnp.sum(probs * prob_grad, axis=-1, keepdims=True)
    score_grad = (probs * (prob_grad - centre) * scale).astype(jnp.bfloat16)
    rotated_grad = jnp.einsum(
        "kgij,ikgd->jkd", score_grad, query_g, preferred_element_type=jnp.float32
    )
    key_grad = rotated_grad * cosine[:, None, :] + rotate_back(rotated_grad * sine[:, None, :])
    return (key_grad.astype(jnp.bfloat16), value_grad)


def norm_backward(normed_grad, gain_f, nhat, inv_rms):
    gain_grad_in = normed_grad * gain_f
    centre = jnp.mean(gain_grad_in * nhat, axis=-1, keepdims=True)
    return ((gain_grad_in - nhat * centre) * inv_rms).astype(jnp.bfloat16)


def on_device(
    hidden_states,
    norm_gain,
    key_weight,
    value_weight,
    queries,
    context_cotangent,
    lengths,
    policy_logp,
    reference_logp,
):
    both_full = lax.all_gather(
        jnp.stack([key_weight[0], value_weight[0]]), "dp", axis=1, tiled=True
    )
    key_full, value_full = (both_full[0], both_full[1])
    hidden = hidden_states[0]
    gain_f = norm_gain[0].astype(jnp.float32)
    tok_rows = hidden.shape[0]
    seq_count = lengths.shape[1]
    seq_len = tok_rows // seq_count
    kv_cols = key_full.shape[1]
    kv_local = kv_cols // HD
    q_local = queries.shape[2] // HD
    hidden_f = hidden.astype(jnp.float32)
    inv_rms = lax.rsqrt(jnp.mean(hidden_f * hidden_f, axis=-1, keepdims=True) + norm_eps)
    nhat = hidden_f * inv_rms
    normed = (nhat * gain_f).astype(jnp.bfloat16)
    projected = jnp.einsum("td,wdc->wtc", normed, both_full, preferred_element_type=jnp.float32)
    key_raw = projected[0]
    values = projected[1].astype(jnp.bfloat16)
    cosine, sine = rope_tables(seq_len, HD)
    key_four = key_raw.reshape(seq_count, seq_len, kv_local, HD)
    keys = (
        key_four * cosine[None, :, None, :] + rotate_half(key_four) * sine[None, :, None, :]
    ).astype(jnp.bfloat16)
    total_seqs = seq_count * lax.axis_size("dp")
    seq_weight = 2.0 * jax.nn.sigmoid(npo_beta * (policy_logp[0] - reference_logp[0])) / total_seqs
    live = jnp.arange(seq_len)[None, :] < lengths[0][:, None]
    factor = jnp.where(live, seq_weight[:, None], 0.0)
    scaled = (
        context_cotangent[0].reshape(seq_count, seq_len, q_local, HD).astype(jnp.float32)
        * factor[:, :, None, None]
    ).astype(jnp.bfloat16)

    def one_sequence(items):
        return sequence_grads(items[0], items[1], items[2], items[3], items[4], cosine, sine)

    key_grad, value_grad = lax.map(
        one_sequence,
        (
            queries[0].reshape(seq_count, seq_len, q_local, HD),
            keys,
            values.reshape(seq_count, seq_len, kv_local, HD),
            scaled,
            lengths[0],
        ),
    )
    key_grad = key_grad.reshape(tok_rows, kv_cols)
    value_grad = value_grad.reshape(tok_rows, kv_cols)
    combined = jnp.concatenate([key_grad, value_grad], axis=1)
    grad_total = lax.psum_scatter(
        lax.dot_general(
            normed, combined, (((0,), (0,)), ((), ())), preferred_element_type=jnp.float32
        ).astype(jnp.bfloat16),
        "dp",
        scatter_dimension=0,
        tiled=True,
    )
    both_grads = jnp.stack([key_grad, value_grad])
    n_pipe = lax.axis_size("pipe")
    n_tensor = lax.axis_size("tensor")
    sizes = [tok_rows // 4, tok_rows * 5 // 16, tok_rows * 5 // 16, tok_rows // 8]
    bounds = [sum(sizes[:c]) for c in range(len(sizes) + 1)]
    chunks = len(sizes)
    exchange_steps = [
        [
            (p * n_tensor + t, p * n_tensor + (t + step) % n_tensor)
            for p in range(1, n_pipe)
            for t in range(n_tensor)
        ]
        for step in range(1, n_tensor)
    ]
    shift_pairs = [
        ((p + 1) * n_tensor + (t if (p + 1) // 2 == p // 2 else n_tensor - 1 - t), p * n_tensor + t)
        for p in range(n_pipe - 1)
        for t in range(n_tensor)
    ]
    lowers = []
    held = None
    for c in range(chunks):
        sl = slice(bounds[c], bounds[c + 1])
        part = jnp.einsum(
            "wtc,wdc->td", both_grads[:, sl], both_full, preferred_element_type=jnp.float32
        )
        part_low = part.astype(jnp.bfloat16)
        if held is not None:
            if len(lowers) > 0:
                part_low, held, lowers[-1] = lax.optimization_barrier((part_low, held, lowers[-1]))
            else:
                part_low, held = lax.optimization_barrier((part_low, held))
            lowers.append(lax.ppermute(held, ("pipe", "tensor"), shift_pairs))
        normed_grad = part_low.astype(jnp.float32)
        for pairs in exchange_steps:
            normed_grad = normed_grad + lax.ppermute(part_low, ("pipe", "tensor"), pairs).astype(
                jnp.float32
            )
        held = norm_backward(normed_grad, gain_f, nhat[sl], inv_rms[sl])
    lowers.append(lax.ppermute(held, ("pipe", "tensor"), shift_pairs))
    lower = jnp.concatenate(lowers, axis=0)
    return (grad_total[:, :kv_cols][None], grad_total[:, kv_cols:][None], lower[None])


def solution(mesh):
    in_specs = (
        P("pipe", "dp", None),
        P("pipe", None),
        P("pipe", "dp", "tensor"),
        P("pipe", "dp", "tensor"),
        P("pipe", "dp", "tensor"),
        P("pipe", "dp", "tensor"),
        P("pipe", "dp"),
        P("pipe", "dp"),
        P("pipe", "dp"),
    )
    out_specs = (P("pipe", "dp", "tensor"), P("pipe", "dp", "tensor"), P("pipe", "dp", None))
    return jax.shard_map(
        on_device, mesh=mesh, in_specs=in_specs, out_specs=out_specs, check_vma=False
    )
```

profile of v0, /device:TPU:1, one launch (start us, length us, event | category | flops | bytes accessed | tf_op | source)
XLA Modules:
  0.0 254.6 jit_solution(5297577957536231163)
XLA Ops:
  17.3 3.1 %fusion.6 = f32[256]{0:T(256)S(1)} fusion(bf16[1,256,8192]{2,1,0:T(8,128)(2,1)} %param.9), kind=kLoop, calls=%fused_computation.13 | loop fusion | flops 6291200 | bytes 4195328 | tf_op jit(solution)/shard_map/reduce_sum | solution.py:99
  20.5 71.1 %all-gather.2.cloned.1.call-done = bf16[2,8192,256]{1,2,0:T(8,128)(2,1)} async-done(((bf16[2,512,256]{1,2,0:T(8,128)(2,1)}), bf16[2,8192,256]{1,2,0:T(8,128)(2,1)}) %all-gather.2.cloned.1.call-update) | async-done | bytes 8388624 | tf_op jit(solution)/shard_map/all_gather | solution.py:86
  91.7 7.0 %fusion.20 = f32[2,256,256]{1,2,0:T(8,128)S(1)} fusion(bf16[2,8192,256]{1,2,0:T(8,128)(2,1)} %all-gather.2.cloned.1.call-done, f32[8192]{0:T(1024)S(1)} %bitcast.125, bf16[1,256,8192]{2,1,0:T(8,128)(2,1)} %param.9, f32[256]{0:T(256)S(1)} %add_rsqrt_fusion), kind=kOutput, calls=%fused_computation.44 | convolution fusion | flops 2155872256 | bytes 13140992 | tf_op jit(solution)/shard_map/td,wdc->wtc/dot_general | solution.py:102
  99.9 5.3 %fusion.60 = (f32[2,8,256]{2,1,0:T(8,128)S(1)}, f32[2,8,256,256]{2,3,1,0:T(8,128)}) fusion(pred[256,256]{0,1:T(8,128)(4,1)S(1)} %fusion.39, bf16[256,2,8,128]{0,3,2,1:T(8,128)(2,1)} %bitcast.137, f32[256,2,64]{2,0,1:T(8,128)S(1)} %bitcast.142, f32[256,2,64]{2,0,1:T(8,128)} %negate_bitcast_fusion, f32[256,2,128]{2,0,1:T(8,128)S(1)} %copy.15, ...), kind=kOutput, calls=%fused_computation.107 | convolution fusion | flops 274006272 | bytes 6111232 | tf_op jit(solution)/shard_map/while/body/eval_jaxpr/sub | solution.py:53
  105.1 3.0 %fusion.27 = bf16[2,128,256]{2,1,0:T(8,128)(2,1)S(1)} fusion(f32[256,2,8,128]{0,3,2,1:T(8,128)S(1)} %bitcast.123, f32[256]{0:T(256)S(1)} %broadcast_select_fusion, f32[2,8,256,256]{2,3,1,0:T(8,128)} %get-tuple-element.60, f32[2,8,256]{2,1,0:T(8,128)S(1)} %get-tuple-element.59), kind=kOutput, calls=%fused_computation.47 | convolution fusion | flops 271646720 | bytes 6439936 | tf_op jit(solution)/shard_map/while/body/eval_jaxpr/kgij,ikgd->jkd/dot_general | solution.py:56
  108.3 2.7 %fusion.30 = f32[2,256,256,8]{2,1,3,0:T(8,128)} fusion(bf16[256,2,128,1]{0,2,3,1:T(8,128)(2,1)S(1)} %bitcast.139, f32[256,2,8,128]{0,3,2,1:T(8,128)S(1)} %bitcast.124, f32[256]{0:T(256)S(1)} %broadcast_select_fusion), kind=kOutput, calls=%fused_computation.52 | convolution fusion | flops 269484032 | bytes 6423552 | tf_op jit(solution)/shard_map/while/body/eval_jaxpr/ikgd,jkd->kgij/dot_general | solution.py:59
  111.0 7.5 %fusion.23 = f32[2,256,128]{1,2,0:T(8,128)S(1)} fusion(bf16[256,2,8,128]{0,3,2,1:T(8,128)(2,1)} %bitcast.138, f32[2,256,256,8]{2,1,3,0:T(8,128)} %fusion.30, f32[2,8,256,256]{2,3,1,0:T(8,128)} %get-tuple-element.60, f32[2,8,256]{2,1,0:T(8,128)S(1)} %get-tuple-element.59), kind=kOutput, calls=%fused_computation.45 | convolution fusion | flops 275779840 | bytes 9715712 | tf_op jit(solution)/shard_map/while/body/eval_jaxpr/kgij,ikgd->jkd/dot_general | solution.py:62
  118.7 5.1 %fusion.4 = bf16[64,8192]{1,0:T(8,128)(2,1)S(1)} fusion(bf16[2,8192,256]{1,2,0:T(8,128)(2,1)} %all-gather.2.cloned.1.call-done, bf16[1,256,256]{2,1,0:T(8,128)(2,1)S(1)} %copy.26, bf16[1,256,256]{2,1,0:T(8,128)(2,1)S(1)} %copy.27), kind=kOutput, calls=%fused_computation.10 | convolution fusion | flops 537427968 | bytes 9699328 | tf_op jit(solution)/shard_map/wtc,wdc->td/dot_general | solution.py:166
  123.8 3.3 %collective-permute-start = (bf16[64,8192]{1,0:T(8,128)(2,1)S(1)}, bf16[64,8192]{1,0:T(8,128)(2,1)S(1)}, u32[]{:S(2)}, u32[]{:S(2)}) collective-permute-start(bf16[64,8192]{1,0:T(8,128)(2,1)S(1)} %fusion.4), channel_id=1, source_target_pairs={{32,33},{33,32},{64,65},{65,64},{96,97},{97,96},{34,35},{35,34},{6... | collective-permute-start | bytes 3145736 | tf_op jit(solution)/shard_map/ppermute | solution.py:178
  127.1 5.8 %convolution_convert_fusion = bf16[8192,512]{1,0:T(8,128)(2,1)} fusion(f32[8192]{0:T(1024)S(1)} %bitcast.126, bf16[256,256]{0,1:T(8,128)(2,1)S(1)} %bitcast.144, bf16[256,256]{0,1:T(8,128)(2,1)S(1)} %bitcast.141, bf16[1,256,8192]{2,1,0:T(8,128)(2,1)S(1)} %copy-done, f32[256]{0:T(256)S(1)} %add_rsqrt_fusion), kind=kOutput, calls=%fused_computation.2 | convolution fusion | flops 2160590848 | bytes 12878848 | tf_op jit(solution)/shard_map/dot_general | solution.py:136
  132.9 3.3 %convert_multiply_fusion = f32[256,8192]{1,0:T(8,128)S(1)} fusion(bf16[1,256,8192]{2,1,0:T(8,128)(2,1)} %param.9, f32[256]{0:T(256)S(1)} %add_rsqrt_fusion), kind=kLoop, calls=%fused_computation.3 | loop fusion | flops 4194304 | bytes 12583936 | tf_op jit(solution)/shard_map/mul | solution.py:100
  136.2 5.1 %fusion.3 = bf16[80,8192]{1,0:T(8,128)(2,1)S(1)} fusion(bf16[2,8192,256]{1,2,0:T(8,128)(2,1)} %all-gather.2.cloned.1.call-done, bf16[1,256,256]{2,1,0:T(8,128)(2,1)S(1)} %copy.26, bf16[1,256,256]{2,1,0:T(8,128)(2,1)S(1)} %copy.27), kind=kOutput, calls=%fused_computation.9 | convolution fusion | flops 671784960 | bytes 9961472 | tf_op jit(solution)/shard_map/wtc,wdc->td/dot_general | solution.py:166
  142.6 2.2 collective-permute-start.1
  146.4 1.9 collective-permute-start.2
  148.4 13.0 %collective-permute-done.1 = bf16[80,8192]{1,0:T(8,128)(2,1)S(1)} collective-permute-done((bf16[80,8192]{1,0:T(8,128)(2,1)S(1)}, bf16[80,8192]{1,0:T(8,128)(2,1)S(1)}, u32[]{:S(2)}, u32[]{:S(2)}) %collective-permute-start.1) | collective-permute-done | bytes 1310752 | tf_op jit(solution)/shard_map/ppermute | solution.py:178
  162.7 11.2 %collective-permute-done.2 = bf16[64,8192]{1,0:T(8,128)(2,1)S(1)} collective-permute-done((bf16[64,8192]{1,0:T(8,128)(2,1)S(1)}, bf16[64,8192]{1,0:T(8,128)(2,1)S(1)}, u32[]{:S(2)}, u32[]{:S(2)}) %collective-permute-start.2) | collective-permute-done | bytes 1048608 | tf_op jit(solution)/shard_map/ppermute | solution.py:175
  173.9 2.2 collective-permute-start.3
  177.7 1.9 collective-permute-start.4
  179.6 13.0 %collective-permute-done.3 = bf16[80,8192]{1,0:T(8,128)(2,1)S(1)} collective-permute-done((bf16[80,8192]{1,0:T(8,128)(2,1)S(1)}, bf16[80,8192]{1,0:T(8,128)(2,1)S(1)}, u32[]{:S(2)}, u32[]{:S(2)}) %collective-permute-start.3) | collective-permute-done | bytes 1310752 | tf_op jit(solution)/shard_map/ppermute | solution.py:178
  194.1 14.7 %collective-permute-done.4 = bf16[80,8192]{1,0:T(8,128)(2,1)S(1)} collective-permute-done((bf16[80,8192]{1,0:T(8,128)(2,1)S(1)}, bf16[80,8192]{1,0:T(8,128)(2,1)S(1)}, u32[]{:S(2)}, u32[]{:S(2)}) %collective-permute-start.4) | collective-permute-done | bytes 1310752 | tf_op jit(solution)/shard_map/ppermute | solution.py:175
  208.7 2.2 collective-permute-start.6
  212.9 5.7 %collective-permute-done.6 = bf16[32,8192]{1,0:T(8,128)(2,1)S(1)} collective-permute-done((bf16[32,8192]{1,0:T(8,128)(2,1)S(1)}, bf16[32,8192]{1,0:T(8,128)(2,1)S(1)}, u32[]{:S(2)}, u32[]{:S(2)}) %collective-permute-start.6) | collective-permute-done | bytes 524320 | tf_op jit(solution)/shard_map/ppermute | solution.py:178
  221.2 22.6 %collective-permute-done.7 = bf16[32,8192]{1,0:T(8,128)(2,1)S(1)} collective-permute-done((bf16[32,8192]{1,0:T(8,128)(2,1)S(1)}, bf16[32,8192]{1,0:T(8,128)(2,1)S(1)}, u32[]{:S(2)}, u32[]{:S(2)}) %collective-permute-start.7) | collective-permute-done | bytes 524320 | tf_op jit(solution)/shard_map/ppermute | solution.py:182
  243.8 2.1 maximum_bitcast_fusion
  (69 shorter events, 23.2 us)
Async XLA Ops:
  7.2 7.3 %copy-start.1 = (bf16[1,256,2048]{2,1,0:T(8,128)(2,1)S(1)}, bf16[1,256,2048]{2,1,0:T(8,128)(2,1)}, u32[]{:S(2)}) copy-start(bf16[1,256,2048]{2,1,0:T(8,128)(2,1)} %param.13) | copy-start | bytes 3145732
  7.2 84.5 %all-gather.2.cloned.1.call-start = ((), (), s32[]{:S(2)}) async-start(), calls=%async_computation.1 | async-start | bytes 8912896 | tf_op jit(solution)/shard_map/all_gather | solution.py:86
  10.4 235.6 %reduce-scatter.2.cloned.1.call-start = ((), (), s32[]{:S(2)}) async-start(), calls=%async_computation.2 | async-start | bytes 8912896 | tf_op jit(solution)/shard_map/reduce_scatter | solution.py:135
  20.4 115.8 %copy-start.2 = (f32[256]{0:T(256)}, f32[256]{0:T(256)S(1)}, u32[]{:S(2)}) copy-start(f32[256]{0:T(256)S(1)} %add_rsqrt_fusion) | copy-start | bytes 3076
  118.7 8.4 %copy-start = (bf16[1,256,8192]{2,1,0:T(8,128)(2,1)S(1)}, bf16[1,256,8192]{2,1,0:T(8,128)(2,1)}, u32[]{:S(2)}) copy-start(bf16[1,256,8192]{2,1,0:T(8,128)(2,1)} %param.9) | copy-start | bytes 12582916
  123.8 17.5 %collective-permute-start = (bf16[64,8192]{1,0:T(8,128)(2,1)S(1)}, bf16[64,8192]{1,0:T(8,128)(2,1)S(1)}, u32[]{:S(2)}, u32[]{:S(2)}) collective-permute-start(bf16[64,8192]{1,0:T(8,128)(2,1)S(1)} %fusion.4), channel_id=1, source_target_pairs={{32,33},{33,32},{64,65},{65,64},{96,97},{97,96},{34,35},{35,34},{6... | collective-permute-start | bytes 3145736 | tf_op jit(solution)/shard_map/ppermute | solution.py:178
  136.2 8.7 %slice-start = ((s8[8388608]{0:T(1024)(128)(4,1)}), s8[4194304]{0:T(1024)(128)(4,1)S(1)}, s32[]{:S(2)}) async-start(s8[8388608]{0:T(1024)(128)(4,1)} %bitcast.121), calls=%async_computation.3 | async-start | bytes 8388608
  136.2 8.7 %slice-start.1 = ((s8[8388608]{0:T(1024)(128)(4,1)}), s8[4194304]{0:T(1024)(128)(4,1)S(1)}, s32[]{:S(2)}) async-start(s8[8388608]{0:T(1024)(128)(4,1)} %bitcast.121), calls=%async_computation.4 | async-start | bytes 8388608
  141.3 0.7 slice-start.2
  141.3 3.5 %copy-start.3 = (f32[256]{0:T(256)S(1)}, f32[256]{0:T(256)}, u32[]{:S(2)}) copy-start(f32[256]{0:T(256)} %copy-done.2) | copy-start | bytes 3076
  142.6 18.8 %collective-permute-start.1 = (bf16[80,8192]{1,0:T(8,128)(2,1)S(1)}, bf16[80,8192]{1,0:T(8,128)(2,1)S(1)}, u32[]{:S(2)}, u32[]{:S(2)}) collective-permute-start(bf16[80,8192]{1,0:T(8,128)(2,1)S(1)} %fusion.3), channel_id=1, source_target_pairs={{32,33},{33,32},{64,65},{65,64},{96,97},{97,96},{34,35},{35,34},{6... | collective-permute-start | bytes 3932168 | tf_op jit(solution)/shard_map/ppermute | solution.py:178
  146.4 27.5 %collective-permute-start.2 = (bf16[64,8192]{1,0:T(8,128)(2,1)S(1)}, bf16[64,8192]{1,0:T(8,128)(2,1)S(1)}, u32[]{:S(2)}, u32[]{:S(2)}) collective-permute-start(bf16[64,8192]{1,0:T(8,128)(2,1)S(1)} %multiply_convert_fusion.3), channel_id=1, source_target_pairs={{32,0},{33,1},{65,32},{64,33},{96,64},{97,65},{34,2},{35,3},{67,34... | collective-permute-start | bytes 3145736 | tf_op jit(solution)/shard_map/ppermute | solution.py:175
  173.9 18.7 %collective-permute-start.3 = (bf16[80,8192]{1,0:T(8,128)(2,1)S(1)}, bf16[80,8192]{1,0:T(8,128)(2,1)S(1)}, u32[]{:S(2)}, u32[]{:S(2)}) collective-permute-start(bf16[80,8192]{1,0:T(8,128)(2,1)S(1)} %fusion.2), channel_id=1, source_target_pairs={{32,33},{33,32},{64,65},{65,64},{96,97},{97,96},{34,35},{35,34},{6... | collective-permute-start | bytes 3932168 | tf_op jit(solution)/shard_map/ppermute | solution.py:178
  177.7 31.1 %collective-permute-start.4 = (bf16[80,8192]{1,0:T(8,128)(2,1)S(1)}, bf16[80,8192]{1,0:T(8,128)(2,1)S(1)}, u32[]{:S(2)}, u32[]{:S(2)}) collective-permute-start(bf16[80,8192]{1,0:T(8,128)(2,1)S(1)} %multiply_convert_fusion.2), channel_id=1, source_target_pairs={{32,0},{33,1},{65,32},{64,33},{96,64},{97,65},{34,2},{35,3},{67,34... | collective-permute-start | bytes 3932168 | tf_op jit(solution)/shard_map/ppermute | solution.py:175
  208.7 9.9 %collective-permute-start.6 = (bf16[32,8192]{1,0:T(8,128)(2,1)S(1)}, bf16[32,8192]{1,0:T(8,128)(2,1)S(1)}, u32[]{:S(2)}, u32[]{:S(2)}) collective-permute-start(bf16[32,8192]{1,0:T(8,128)(2,1)S(1)} %fusion.5), channel_id=1, source_target_pairs={{32,33},{33,32},{64,65},{65,64},{96,97},{97,96},{34,35},{35,34},{6... | collective-permute-start | bytes 1572872 | tf_op jit(solution)/shard_map/ppermute | solution.py:178
  211.0 32.8 %collective-permute-start.5 = (bf16[80,8192]{1,0:T(8,128)(2,1)S(1)}, bf16[80,8192]{1,0:T(8,128)(2,1)S(1)}, u32[]{:S(2)}, u32[]{:S(2)}) collective-permute-start(bf16[80,8192]{1,0:T(8,128)(2,1)S(1)} %multiply_convert_fusion.1), channel_id=1, source_target_pairs={{32,0},{33,1},{65,32},{64,33},{96,64},{97,65},{34,2},{35,3},{67,34... | collective-permute-start | bytes 3932168 | tf_op jit(solution)/shard_map/ppermute | solution.py:175
  219.3 24.5 %collective-permute-start.7 = (bf16[32,8192]{1,0:T(8,128)(2,1)S(1)}, bf16[32,8192]{1,0:T(8,128)(2,1)S(1)}, u32[]{:S(2)}, u32[]{:S(2)}) collective-permute-start(bf16[32,8192]{1,0:T(8,128)(2,1)S(1)} %multiply_convert_fusion.7), channel_id=1, source_target_pairs={{32,0},{33,1},{65,32},{64,33},{96,64},{97,65},{34,2},{35,3},{67,34... | collective-permute-start | bytes 1572872 | tf_op jit(solution)/shard_map/ppermute | solution.py:182
Sparse Core Ops, SparseCore 0:
  10.7 80.9 all-gather.1
  133.0 84.3 reduce-scatter.1
where the time goes:
time: 255 us
  waiting for transfers between devices  151 us (59%)
  matrix products  44.6 us (17%)
  starting transfers between devices  17.6 us (7%)
  between operations  16.5 us (6%)
  other arithmetic  16 us (6%)
  local copies, waits for them, and re-layouts  8.69 us (3%)
    all_gather x1, waiting for transfers between devices, on_device(): lax.all_gather(jnp.stack([key_weight[0], value_weight[0]]), 'dp', axis=1,...  71.1 us
    ppermute x4, waiting for transfers between devices, on_device(): lowers.append(lax.ppermute(held, ('pipe', 'tensor'), shift_pairs))  48.4 us
    ppermute x4, waiting for transfers between devices, on_device(): lax.ppermute(part_low, ('pipe', 'tensor'), pairs).astype(jnp.float32)  31.7 us
    dot_general x4, matrix products, on_device(): jnp.einsum('wtc,wdc->td', both_grads[:, sl], both_full, preferred_element...  13.3 us
    ppermute x4, starting transfers between devices, on_device(): lax.ppermute(part_low, ('pipe', 'tensor'), pairs).astype(jnp.float32)  9.85 us
    ppermute x4, starting transfers between devices, on_device(): lowers.append(lax.ppermute(held, ('pipe', 'tensor'), shift_pairs))  7.67 us
    dot_general x1, matrix products, sequence_grads(): jnp.einsum('kgij,ikgd->jkd', score_grad, query_g, preferred_element_type=...  7.48 us
    dot_general x1, matrix products, on_device(): jnp.einsum('td,wdc->wtc', normed, both_full, preferred_element_type=jnp.f...  7.02 us
  transfers between devices with their start and end apart: 10, of which 7 were waited for; matrix products, arithmetic and copies ran while one was open for 13% of the time, Pallas kernels for 0%

commit v1 on v0

--- a/solution.py
+++ b/solution.py
@@ -83,8 +83,14 @@
     policy_logp,
     reference_logp,
 ):
-    both_full = lax.all_gather(
-        jnp.stack([key_weight[0], value_weight[0]]), "dp", axis=1, tiled=True
+    both_full = jnp.concatenate(
+        lax.all_to_all(
+            jnp.stack([jnp.stack([key_weight[0], value_weight[0]])] * lax.axis_size("dp")),
+            "dp",
+            0,
+            0,
+        ),
+        axis=1,
     )
     key_full, value_full = (both_full[0], both_full[1])
     hidden = hidden_states[0]

time: 255 us -> 338 us (1.33)
  waiting for transfers between devices: 151 us -> 213 us
  local copies, waits for them, and re-layouts: 8.69 us -> 20.2 us
  starting transfers between devices: 17.6 us -> 26.6 us
    all_to_all x0 -> x1, waiting for transfers between devices: none -> 135 us  [on_device(): lax.all_to_all(jnp.stack([jnp.stack([key_weight[0], value_weight[0]])] *...]
    all_gather x1 -> x0, waiting for transfers between devices: 71.1 us -> none  [on_device(): lax.all_gather(jnp.stack([key_weight[0], value_weight[0]]), 'dp', axis=1,...]
    all_to_all x0 -> x1, starting transfers between devices: none -> 8.78 us  [on_device(): lax.all_to_all(jnp.stack([jnp.stack([key_weight[0], value_weight[0]])] *...]
    reshape x0 -> x1, local copies, waits for them, and re-layouts: none -> 8 us  [on_device(): jnp.concatenate(lax.all_to_all(jnp.stack([jnp.stack([key_weight[0], value...]
    another operation x0 -> x2, local copies, waits for them, and re-layouts: none -> 4.4 us  [the longest x1 4.19 us: on_device(): jnp.stack([jnp.stack([key_weight[0], value_weight[0]])] * lax.axis_size('...]
  transfers between devices with their start and end apart: 10 -> 10, of which waited for: 7 -> 7; matrix products, arithmetic and copies ran while one was open for 13% -> 10% of each run, Pallas kernels for 0% -> 0%
where the time goes in v1:
time: 338 us; the launch traced here: 336 us
  waiting for transfers between devices  213 us (63%)
  matrix products  43.5 us (13%)
  starting transfers between devices  26.6 us (8%)
  local copies, waits for them, and re-layouts  20.2 us (6%)
  between operations  16.5 us (5%)
  other arithmetic  15.7 us (5%)
    all_to_all x1, waiting for transfers between devices, on_device(): lax.all_to_all(jnp.stack([jnp.stack([key_weight[0], value_weight[0]])] *...  135 us
    ppermute x4, waiting for transfers between devices, on_device(): lowers.append(lax.ppermute(held, ('pipe', 'tensor'), shift_pairs))  45.8 us
    ppermute x4, waiting for transfers between devices, on_device(): lax.ppermute(part_low, ('pipe', 'tensor'), pairs).astype(jnp.float32)  31.9 us
    dot_general x4, matrix products, on_device(): jnp.einsum('wtc,wdc->td', both_grads[:, sl], both_full, preferred_element...  13.3 us
    ppermute x4, starting transfers between devices, on_device(): lax.ppermute(part_low, ('pipe', 'tensor'), pairs).astype(jnp.float32)  10.2 us
    all_to_all x1, starting transfers between devices, on_device(): lax.all_to_all(jnp.stack([jnp.stack([key_weight[0], value_weight[0]])] *...  8.78 us
    reshape x1, local copies, waits for them, and re-layouts, on_device(): jnp.concatenate(lax.all_to_all(jnp.stack([jnp.stack([key_weight[0], value...  8 us
    ppermute x4, starting transfers between devices, on_device(): lowers.append(lax.ppermute(held, ('pipe', 'tensor'), shift_pairs))  7.67 us
  transfers between devices with their start and end apart: 10, of which 7 were waited for; matrix products, arithmetic and copies ran while one was open for 10% of the time, Pallas kernels for 0%

profile of v1, /device:TPU:1, one launch (start us, length us, event | category | flops | bytes accessed | tf_op | source)
XLA Modules:
  0.0 335.8 jit_solution(13456269614851034239)
XLA Ops:
  8.5 4.2 %stack.7 = bf16[16,2,512,256]{2,3,1,0:T(8,128)(2,1)} broadcast(bf16[2,512,256]{1,2,0:T(8,128)(2,1)S(1)} %copy.31), dimensions={1,2,3} | broadcast | bytes 8912896 | tf_op jit(solution)/shard_map/stack | solution.py:88
  12.7 8.8 %all-to-all-start = ((bf16[16,2,512,256]{2,3,1,0:T(8,128)(2,1)}), bf16[16,2,512,256]{2,3,1,0:T(8,128)(2,1)}, u32[]{:S(2)}, u32[]{:S(2)}) async-start(bf16[16,2,512,256]{2,3,1,0:T(8,128)(2,1)} %stack.7), calls=%async_computation | async-start | bytes 16777216 | tf_op jit(solution)/shard_map/all_to_all | solution.py:87
  28.2 3.1 fusion.8
  32.1 135.5 %all-to-all-done = bf16[16,2,512,256]{2,3,1,0:T(8,128)(2,1)} async-done(((bf16[16,2,512,256]{2,3,1,0:T(8,128)(2,1)}), bf16[16,2,512,256]{2,3,1,0:T(8,128)(2,1)}, u32[]{:S(2)}, u32[]{:S(2)}) %all-to-all-start) | async-done | bytes 8388640 | tf_op jit(solution)/shard_map/all_to_all | solution.py:87
  167.6 8.0 %copy.68 = bf16[16,2,32,8,512]{4,3,0,2,1:T(8,128)(2,1)} copy(bf16[16,2,32,8,512]{4,3,2,1,0:T(8,128)(2,1)} %bitcast.44) | data formatting | bytes 16777216 | tf_op jit(solution)/shard_map/reshape | solution.py:86
  175.6 5.8 %fusion.28 = f32[2,256,256]{1,2,0:T(8,128)S(1)} fusion(bf16[2,8192,256]{1,2,0:T(8,128)(2,1)} %bitcast.126, bf16[1,256,8192]{2,1,0:T(8,128)(2,1)S(1)} %copy-done, f32[8192]{0:T(1024)S(1)} %bitcast.135, f32[256]{0:T(256)S(1)} %add_rsqrt_fusion), kind=kOutput, calls=%fused_computation.51 | convolution fusion | flops 2155872256 | bytes 13140992 | tf_op jit(solution)/shard_map/td,wdc->wtc/dot_general | solution.py:108
  182.6 5.3 %fusion.69 = (f32[2,8,256]{2,1,0:T(8,128)S(1)}, f32[2,8,256,256]{2,3,1,0:T(8,128)}) fusion(pred[256,256]{0,1:T(8,128)(4,1)} %fusion.47, bf16[256,2,8,128]{0,3,2,1:T(8,128)(2,1)} %bitcast.147, f32[256,2,64]{2,0,1:T(8,128)S(1)} %bitcast.152, f32[256,2,64]{2,0,1:T(8,128)} %negate_bitcast_fusion, f32[256,2,128]{2,0,1:T(8,128)S(1)} %copy.34, ...), kind=kOutput, calls=%fused_computation.114 | convolution fusion | flops 274006272 | bytes 6111232 | tf_op jit(solution)/shard_map/while/body/eval_jaxpr/sub | solution.py:53
  187.9 3.1 fusion.35
  191.6 2.7 fusion.38
  194.4 7.5 %fusion.31 = f32[2,256,128]{1,2,0:T(8,128)S(1)} fusion(bf16[256,2,8,128]{0,3,2,1:T(8,128)(2,1)} %bitcast.148, f32[2,256,256,8]{2,1,3,0:T(8,128)} %fusion.38, f32[2,8,256,256]{2,3,1,0:T(8,128)} %get-tuple-element.60, f32[2,8,256]{2,1,0:T(8,128)S(1)} %get-tuple-element.59), kind=kOutput, calls=%fused_computation.52 | convolution fusion | flops 275779840 | bytes 9715712 | tf_op jit(solution)/shard_map/while/body/eval_jaxpr/kgij,ikgd->jkd/dot_general | solution.py:62
  202.1 5.1 %fusion.6 = bf16[64,8192]{1,0:T(8,128)(2,1)S(1)} fusion(bf16[2,8192,256]{1,2,0:T(8,128)(2,1)} %bitcast.127, bf16[1,256,256]{2,1,0:T(8,128)(2,1)S(1)} %copy.45, bf16[1,256,256]{2,1,0:T(8,128)(2,1)S(1)} %copy.46), kind=kOutput, calls=%fused_computation.12 | convolution fusion | flops 537427968 | bytes 9699328 | tf_op jit(solution)/shard_map/wtc,wdc->td/dot_general | solution.py:172
  207.2 3.3 collective-permute-start
  210.5 5.8 %convolution_convert_fusion = bf16[8192,512]{1,0:T(8,128)(2,1)} fusion(f32[8192]{0:T(1024)S(1)} %bitcast.136, bf16[256,256]{0,1:T(8,128)(2,1)S(1)} %bitcast.154, bf16[256,256]{0,1:T(8,128)(2,1)S(1)} %bitcast.151, bf16[1,256,8192]{2,1,0:T(8,128)(2,1)S(1)} %copy-done.1, f32[256]{0:T(256)S(1)} %add_rsqrt_fusion), kind=kOutput, calls=%fused_computation.2 | convolution fusion | flops 2160590848 | bytes 12878848 | tf_op jit(solution)/shard_map/dot_general | solution.py:142
  216.4 3.3 fusion.2
  219.7 5.1 %fusion.5 = bf16[80,8192]{1,0:T(8,128)(2,1)S(1)} fusion(bf16[2,8192,256]{1,2,0:T(8,128)(2,1)} %bitcast.128, bf16[1,256,256]{2,1,0:T(8,128)(2,1)S(1)} %copy.45, bf16[1,256,256]{2,1,0:T(8,128)(2,1)S(1)} %copy.46), kind=kOutput, calls=%fused_computation.11 | convolution fusion | flops 671784960 | bytes 9961472 | tf_op jit(solution)/shard_map/wtc,wdc->td/dot_general | solution.py:172
  226.1 2.2 collective-permute-start.1
  231.9 13.0 %collective-permute-done.1 = bf16[80,8192]{1,0:T(8,128)(2,1)S(1)} collective-permute-done((bf16[80,8192]{1,0:T(8,128)(2,1)S(1)}, bf16[80,8192]{1,0:T(8,128)(2,1)S(1)}, u32[]{:S(2)}, u32[]{:S(2)}) %collective-permute-start.1) | collective-permute-done | bytes 1310752 | tf_op jit(solution)/shard_map/ppermute | solution.py:184
  246.2 10.8 %collective-permute-done.2 = bf16[64,8192]{1,0:T(8,128)(2,1)S(1)} collective-permute-done((bf16[64,8192]{1,0:T(8,128)(2,1)S(1)}, bf16[64,8192]{1,0:T(8,128)(2,1)S(1)}, u32[]{:S(2)}, u32[]{:S(2)}) %collective-permute-start.2) | collective-permute-done | bytes 1048608 | tf_op jit(solution)/shard_map/ppermute | solution.py:181
  257.0 2.5 collective-permute-start.3
  263.0 12.7 %collective-permute-done.3 = bf16[80,8192]{1,0:T(8,128)(2,1)S(1)} collective-permute-done((bf16[80,8192]{1,0:T(8,128)(2,1)S(1)}, bf16[80,8192]{1,0:T(8,128)(2,1)S(1)}, u32[]{:S(2)}, u32[]{:S(2)}) %collective-permute-start.3) | collective-permute-done | bytes 1310752 | tf_op jit(solution)/shard_map/ppermute | solution.py:184
  277.1 13.6 %collective-permute-done.4 = bf16[80,8192]{1,0:T(8,128)(2,1)S(1)} collective-permute-done((bf16[80,8192]{1,0:T(8,128)(2,1)S(1)}, bf16[80,8192]{1,0:T(8,128)(2,1)S(1)}, u32[]{:S(2)}, u32[]{:S(2)}) %collective-permute-start.4) | collective-permute-done | bytes 1310752 | tf_op jit(solution)/shard_map/ppermute | solution.py:181
  290.6 2.2 collective-permute-start.6
  294.8 6.1 %collective-permute-done.6 = bf16[32,8192]{1,0:T(8,128)(2,1)S(1)} collective-permute-done((bf16[32,8192]{1,0:T(8,128)(2,1)S(1)}, bf16[32,8192]{1,0:T(8,128)(2,1)S(1)}, u32[]{:S(2)}, u32[]{:S(2)}) %collective-permute-start.6) | collective-permute-done | bytes 524320 | tf_op jit(solution)/shard_map/ppermute | solution.py:184
  303.5 21.4 %collective-permute-done.7 = bf16[32,8192]{1,0:T(8,128)(2,1)S(1)} collective-permute-done((bf16[32,8192]{1,0:T(8,128)(2,1)S(1)}, bf16[32,8192]{1,0:T(8,128)(2,1)S(1)}, u32[]{:S(2)}, u32[]{:S(2)}) %collective-permute-start.7) | collective-permute-done | bytes 524320 | tf_op jit(solution)/shard_map/ppermute | solution.py:188
  (77 shorter events, 28.2 us)
Async XLA Ops:
  12.7 10.9 %copy-start.5 = (bf16[1,8192]{1,0:T(2,128)(2,1)S(1)}, bf16[1,8192]{1,0:T(2,128)(2,1)}, u32[]{:S(2)}) copy-start(bf16[1,8192]{1,0:T(2,128)(2,1)} %param.10) | copy-start | bytes 49156
  12.7 12.8 %copy-start.2 = (bf16[1,256,2048]{2,1,0:T(8,128)(2,1)S(1)}, bf16[1,256,2048]{2,1,0:T(8,128)(2,1)}, u32[]{:S(2)}) copy-start(bf16[1,256,2048]{2,1,0:T(8,128)(2,1)} %param.13) | copy-start | bytes 3145732
  12.7 154.9 %all-to-all-start = ((bf16[16,2,512,256]{2,3,1,0:T(8,128)(2,1)}), bf16[16,2,512,256]{2,3,1,0:T(8,128)(2,1)}, u32[]{:S(2)}, u32[]{:S(2)}) async-start(bf16[16,2,512,256]{2,3,1,0:T(8,128)(2,1)} %stack.7), calls=%async_computation | async-start | bytes 16777216 | tf_op jit(solution)/shard_map/all_to_all | solution.py:87
  21.4 305.6 %reduce-scatter.2.cloned.1.call-start = ((), (), s32[]{:S(2)}) async-start(), calls=%async_computation.2 | async-start | bytes 8912896 | tf_op jit(solution)/shard_map/reduce_scatter | solution.py:141
  31.4 188.3 %copy-start.6 = (f32[256]{0:T(256)}, f32[256]{0:T(256)S(1)}, u32[]{:S(2)}) copy-start(f32[256]{0:T(256)S(1)} %add_rsqrt_fusion) | copy-start | bytes 3076
  167.6 8.0 %copy-start = (bf16[1,256,8192]{2,1,0:T(8,128)(2,1)S(1)}, bf16[1,256,8192]{2,1,0:T(8,128)(2,1)}, u32[]{:S(2)}) copy-start(bf16[1,256,8192]{2,1,0:T(8,128)(2,1)} %param.9) | copy-start | bytes 12582916
  191.0 0.7 copy-start.3
  202.1 8.4 %copy-start.1 = (bf16[1,256,8192]{2,1,0:T(8,128)(2,1)S(1)}, bf16[1,256,8192]{2,1,0:T(8,128)(2,1)}, u32[]{:S(2)}) copy-start(bf16[1,256,8192]{2,1,0:T(8,128)(2,1)} %param.9) | copy-start | bytes 12582916
  202.1 8.4 %copy-start.4 = (bf16[2,128,256]{2,1,0:T(8,128)(2,1)S(1)}, bf16[2,128,256]{2,1,0:T(8,128)(2,1)}, u32[]{:S(2)}) copy-start(bf16[2,128,256]{2,1,0:T(8,128)(2,1)} %copy-done.3) | copy-start | bytes 393220
  207.2 17.6 %collective-permute-start = (bf16[64,8192]{1,0:T(8,128)(2,1)S(1)}, bf16[64,8192]{1,0:T(8,128)(2,1)S(1)}, u32[]{:S(2)}, u32[]{:S(2)}) collective-permute-start(bf16[64,8192]{1,0:T(8,128)(2,1)S(1)} %fusion.6), channel_id=1, source_target_pairs={{32,33},{33,32},{64,65},{65,64},{96,97},{97,96},{34,35},{35,34},{6... | collective-permute-start | bytes 3145736 | tf_op jit(solution)/shard_map/ppermute | solution.py:184
  219.7 8.8 %slice-start = ((s8[8388608]{0:T(1024)(128)(4,1)}), s8[4194304]{0:T(1024)(128)(4,1)S(1)}, s32[]{:S(2)}) async-start(s8[8388608]{0:T(1024)(128)(4,1)} %bitcast.129), calls=%async_computation.3 | async-start | bytes 8388608
  219.7 8.7 %slice-start.1 = ((s8[8388608]{0:T(1024)(128)(4,1)}), s8[4194304]{0:T(1024)(128)(4,1)S(1)}, s32[]{:S(2)}) async-start(s8[8388608]{0:T(1024)(128)(4,1)} %bitcast.129), calls=%async_computation.4 | async-start | bytes 8388608
  224.8 0.8 slice-start.2
  224.8 3.5 %copy-start.7 = (f32[256]{0:T(256)S(1)}, f32[256]{0:T(256)}, u32[]{:S(2)}) copy-start(f32[256]{0:T(256)} %copy-done.6) | copy-start | bytes 3076
  226.1 18.8 %collective-permute-start.1 = (bf16[80,8192]{1,0:T(8,128)(2,1)S(1)}, bf16[80,8192]{1,0:T(8,128)(2,1)S(1)}, u32[]{:S(2)}, u32[]{:S(2)}) collective-permute-start(bf16[80,8192]{1,0:T(8,128)(2,1)S(1)} %fusion.5), channel_id=1, source_target_pairs={{32,33},{33,32},{64,65},{65,64},{96,97},{97,96},{34,35},{35,34},{6... | collective-permute-start | bytes 3932168 | tf_op jit(solution)/shard_map/ppermute | solution.py:184
  230.0 27.0 %collective-permute-start.2 = (bf16[64,8192]{1,0:T(8,128)(2,1)S(1)}, bf16[64,8192]{1,0:T(8,128)(2,1)S(1)}, u32[]{:S(2)}, u32[]{:S(2)}) collective-permute-start(bf16[64,8192]{1,0:T(8,128)(2,1)S(1)} %multiply_convert_fusion.4), channel_id=1, source_target_pairs={{32,0},{33,1},{65,32},{64,33},{96,64},{97,65},{34,2},{35,3},{67,34... | collective-permute-start | bytes 3145736 | tf_op jit(solution)/shard_map/ppermute | solution.py:181
  257.0 18.7 %collective-permute-start.3 = (bf16[80,8192]{1,0:T(8,128)(2,1)S(1)}, bf16[80,8192]{1,0:T(8,128)(2,1)S(1)}, u32[]{:S(2)}, u32[]{:S(2)}) collective-permute-start(bf16[80,8192]{1,0:T(8,128)(2,1)S(1)} %fusion.4), channel_id=1, source_target_pairs={{32,33},{33,32},{64,65},{65,64},{96,97},{97,96},{34,35},{35,34},{6... | collective-permute-start | bytes 3932168 | tf_op jit(solution)/shard_map/ppermute | solution.py:184
  261.1 29.5 %collective-permute-start.4 = (bf16[80,8192]{1,0:T(8,128)(2,1)S(1)}, bf16[80,8192]{1,0:T(8,128)(2,1)S(1)}, u32[]{:S(2)}, u32[]{:S(2)}) collective-permute-start(bf16[80,8192]{1,0:T(8,128)(2,1)S(1)} %multiply_convert_fusion.3), channel_id=1, source_target_pairs={{32,0},{33,1},{65,32},{64,33},{96,64},{97,65},{34,2},{35,3},{67,34... | collective-permute-start | bytes 3932168 | tf_op jit(solution)/shard_map/ppermute | solution.py:181
  290.6 10.3 %collective-permute-start.6 = (bf16[32,8192]{1,0:T(8,128)(2,1)S(1)}, bf16[32,8192]{1,0:T(8,128)(2,1)S(1)}, u32[]{:S(2)}, u32[]{:S(2)}) collective-permute-start(bf16[32,8192]{1,0:T(8,128)(2,1)S(1)} %fusion.7), channel_id=1, source_target_pairs={{32,33},{33,32},{64,65},{65,64},{96,97},{97,96},{34,35},{35,34},{6... | collective-permute-start | bytes 1572872 | tf_op jit(solution)/shard_map/ppermute | solution.py:184
  292.9 32.0 %collective-permute-start.5 = (bf16[80,8192]{1,0:T(8,128)(2,1)S(1)}, bf16[80,8192]{1,0:T(8,128)(2,1)S(1)}, u32[]{:S(2)}, u32[]{:S(2)}) collective-permute-start(bf16[80,8192]{1,0:T(8,128)(2,1)S(1)} %multiply_convert_fusion.2), channel_id=1, source_target_pairs={{32,0},{33,1},{65,32},{64,33},{96,64},{97,65},{34,2},{35,3},{67,34... | collective-permute-start | bytes 3932168 | tf_op jit(solution)/shard_map/ppermute | solution.py:181
  301.5 23.4 %collective-permute-start.7 = (bf16[32,8192]{1,0:T(8,128)(2,1)S(1)}, bf16[32,8192]{1,0:T(8,128)(2,1)S(1)}, u32[]{:S(2)}, u32[]{:S(2)}) collective-permute-start(bf16[32,8192]{1,0:T(8,128)(2,1)S(1)} %multiply_convert_fusion.6), channel_id=1, source_target_pairs={{32,0},{33,1},{65,32},{64,33},{96,64},{97,65},{34,2},{35,3},{67,34... | collective-permute-start | bytes 1572872 | tf_op jit(solution)/shard_map/ppermute | solution.py:188
Sparse Core Ops, SparseCore 0:
  216.5 88.5 reduce-scatter.1
